TPU v7x, 256 devices: a whole 4x4x8 slice. The times are simulated.
256 devices in a mesh: dp: 8 (over z), tm: 32 (over x, y, core).
Axes of the slice: x: 4, y: 4, z: 8, core: 2. Of those that a mesh axis runs over, the one named last changes fastest.
Arguments:
- clips: bfloat16 [8, 128, 16, 16, 128], P('dp', 'tm'), may hold values from -6 to 6
- segment_ids: int32 [8, 128], P('dp'), may hold values from 0 to 3, never falling along the last dimension, each value on 1 to 64 neighbouring positions
- conv_weight: bfloat16 [3456, 128], replicated, may hold values from -0.109375 to 0.109375
- cotangent: bfloat16 [8, 128, 16, 16, 128], P('dp', 'tm'), may hold values from -6 to 6
Outputs:
- activated: bfloat16 [8, 128, 16, 16, 128], P('dp', 'tm')
- grad_clips: bfloat16 [8, 128, 16, 16, 128], P('dp', 'tm')
- grad_weight: float32 [3456, 128], P('tm')
Inputs may be any that keep to these rules, and one draw needn't show every extreme that they name: segment_ids never fall along a sequence; each clip has 1 to 64 frames and one has exactly that many.
All inputs are finite; a program needn't handle non-finite values.
Results may differ from a plain program's by a relative error of at most 0.013.
Values may be sent and summed in bfloat16 or wider, within the bound.
No kernel may reach another device: no remote copies, remote signals or barrier semaphores. Data moves between devices by JAX's collectives and lax.ppermute only.
A program may use at most 64 MiB of HBM per device.

v0:
```python
import jax
import jax.numpy as jnp
from jax import lax
from jax.sharding import PartitionSpec as P


def from_behind(value, axis, steps):
    count = lax.axis_size(axis)
    leading, last = (max(0, -steps), min(count, count - steps))
    return lax.ppermute(value, axis, [(source, source + steps) for source in range(leading, last)])


def per_device(clips, segment_ids, conv_weight, cotangent):
    nfr = clips.shape[1]
    hh = clips.shape[2]
    ww = clips.shape[3]
    cc = clips.shape[4]
    rows = nfr * hh * ww
    earlier = from_behind(clips[:, nfr - 2 :], "tm", 1)
    extended = jnp.concatenate([earlier, clips], axis=1)[0]
    segrow = segment_ids[0]
    segp = jnp.concatenate([jnp.full((2,), -1, jnp.int32), segrow, jnp.full((2,), -2, jnp.int32)])
    start = lax.axis_index("tm") * nfr
    seglocal = lax.dynamic_slice_in_dim(segp, start, nfr + 4, 0)
    own = seglocal[2 : 2 + nfr]
    patches = []
    pre = jnp.zeros((rows, cc), jnp.float32)
    for kt in range(3):
        moved = extended[kt : kt + nfr]
        keep = seglocal[kt : kt + nfr] == own
        moved = jnp.where(keep[:, None, None, None], moved, jnp.zeros_like(moved))
        padded = jnp.pad(moved, ((0, 0), (1, 1), (1, 1), (0, 0)))
        pieces = [padded[:, ky : ky + hh, kx : kx + ww] for ky in range(3) for kx in range(3)]
        patch = jnp.concatenate(pieces, axis=3).reshape(rows, 9 * cc)
        patches.append(patch)
        pre = pre + jnp.dot(
            patch, conv_weight[kt * 9 * cc : (kt + 1) * 9 * cc], preferred_element_type=jnp.float32
        )
    activated = jax.nn.silu(pre).astype(jnp.bfloat16).reshape(clips.shape)
    sig = jax.nn.sigmoid(pre)
    grad_pre = (
        cotangent.reshape(rows, cc).astype(jnp.float32) * sig * (1.0 + pre * (1.0 - sig))
    ).astype(jnp.bfloat16)
    count = lax.axis_size("dp") * lax.axis_size("tm") * rows
    grad_local = jnp.concatenate(
        [
            lax.dot_general(
                patch, grad_pre, (((0,), (0,)), ((), ())), preferred_element_type=jnp.float32
            )
            for patch in patches
        ],
        axis=0,
    )
    grad_local = grad_local / jnp.sqrt(jnp.float32(count))
    frames_grad = grad_pre.reshape(1, nfr, hh, ww, cc)
    later_part = from_behind(frames_grad[:, :2], "tm", -1)
    grad_ext = jnp.concatenate([frames_grad, later_part], axis=1)[0]
    summed = jnp.zeros((rows, 9 * cc), jnp.float32)
    for kt in range(3):
        d = 2 - kt
        later = grad_ext[d : d + nfr]
        keep = seglocal[2 + d : 2 + d + nfr] == own
        later = jnp.where(keep[:, None, None, None], later, jnp.zeros_like(later)).reshape(rows, cc)
        summed = summed + lax.dot_general(
            later,
            conv_weight[kt * 9 * cc : (kt + 1) * 9 * cc],
            (((1,), (1,)), ((), ())),
            preferred_element_type=jnp.float32,
        )
    summed = summed.reshape(nfr, hh, ww, 9, cc)
    canvas = jnp.zeros((nfr, hh + 2, ww + 2, cc), jnp.float32)
    for ky in range(3):
        for kx in range(3):
            canvas = canvas.at[:, ky : ky + hh, kx : kx + ww].add(summed[:, :, :, ky * 3 + kx])
    grad_clips = canvas[:, 1:-1, 1:-1].astype(jnp.bfloat16).reshape(clips.shape)
    share_rows = grad_local.shape[0] // lax.axis_size("tm")
    total = lax.psum(grad_local, ("dp", "tm"))
    grad_weight = lax.dynamic_slice_in_dim(total, lax.axis_index("tm") * share_rows, share_rows, 0)
    return (activated, grad_clips, grad_weight)


def solution(mesh):
    return jax.shard_map(
        per_device,
        mesh=mesh,
        in_specs=(
            P("dp", "tm", None, None, None),
            P("dp", None),
            P(),
            P("dp", "tm", None, None, None),
        ),
        out_specs=(P("dp", "tm", None, None, None), P("dp", "tm", None, None, None), P("tm", None)),
        check_vma=False,
    )
```

profile of v0, /device:TPU:2, one launch (start us, length us, event | category | flops | bytes accessed | tf_op | source)
XLA Modules:
  0.0 301.6 jit_solution(8584760968547292022)
XLA Ops:
  7.2 0.9 slice.482
  8.2 1.9 collective-permute-start
  10.1 0.7 pad_add_fusion
  11.0 2.5 pad_slice_fusion
  14.7 0.7 and_reduce_fusion
  18.7 0.8 fusion.30
  19.5 0.8 convolution_add_fusion.3
  20.5 1.6 fusion.3
  22.1 0.8 fusion.37
  22.9 0.8 fusion.36
  23.7 0.8 fusion.35
  24.6 5.8 %collective-permute-start.1 = (bf16[1,2,16,16,128]{4,3,2,1,0:T(8,128)(2,1)S(1)}, bf16[1,2,16,16,128]{4,3,2,1,0:T(8,128)(2,1)S(1)}, u32[]{:S(2)}, u32[]{:S(2)}) collective-permute-start(bf16[1,2,16,16,128]{4,3,2,1,0:T(8,128)(2,1)S(1)} %slice.545), channel_id=1, source_target_pairs={{1,0},{2,1},{3,2},{4,3},{5,4},{6,5},{7,6},{8,7},{9,8},{10,9},{11,1... | collective-permute-start | bytes 393224 | tf_op jit(solution)/shard_map/ppermute | solution.py:10
  30.4 1.3 maximum_multiply_fusion
  31.7 1.0 collective-permute-done.1
  33.0 0.8 fusion.28
  34.0 0.8 convolution_add_fusion.1
  34.7 3.0 convolution_add_fusion
  37.7 6.9 %reshape.439 = f32[4,16,16,9,128]{4,3,2,1,0:T(8,128)} reshape(f32[1024,1152]{1,0:T(8,128)} %convolution_add_fusion) | data formatting | bytes 9437184 | tf_op jit(solution)/shard_map/reshape | solution.py:70
  44.6 16.6 %fusion.32 = (f32[4,16,16,1,128]{4,3,2,1,0:T(1,128)S(1)}, f32[4,16,16,1,128]{4,3,2,1,0:T(1,128)S(1)}, f32[4,16,16,1,128]{4,3,2,1,0:T(1,128)S(1)}, f32[4,16,16,1,...) fusion(f32[4,16,16,9,128]{4,3,2,1,0:T(8,128)} %reshape.439), kind=kLoop, calls=%fused_computation.101 | loop fusion | bytes 9437184 | tf_op jit(solution)/shard_map/slice | solution.py:74
  61.2 2.2 dynamic-slice_add_fusion
  63.4 4.3 %scatter-add.31 = f32[4,18,18,128]{3,2,1,0:T(8,128)S(1)} dynamic-update-slice(f32[4,18,18,128]{3,2,1,0:T(8,128)S(1)} %scatter-add.30, f32[4,16,16,128]{3,2,1,0:T(8,128)} %dynamic-slice_add_fusion, s32[]{:T(128)} %constant.283.clone.1, s32[]{:T(128)} %bitcast.21, s32[]{:T(128)} %bitcast.22, s32[]{:T(128)} %constant.283.clone.1) | dynamic-update-slice | bytes 1048580 | tf_op jit(solution)/shard_map/scatter-add | solution.py:74
  67.7 3.8 %add_select_fusion = f32[4,16,16,128]{3,2,1,0:T(8,128)} fusion(f32[4,16,16,128]{3,2,1,0:T(8,128)} %bitcast.89, f32[4,18,18,128]{3,2,1,0:T(8,128)S(1)} %scatter-add.31, s32[]{:T(128)} %bitcast.24, s32[]{:T(128)} %bitcast.25, pred[]{:T(512)} %and_reduce_fusion), kind=kLoop, calls=%fused_computation.5 | loop fusion | flops 262144 | bytes 1572873 | tf_op jit(solution)/shard_map/select.11
  71.5 4.3 %scatter-add.34 = f32[4,18,18,128]{3,2,1,0:T(8,128)S(1)} dynamic-update-slice(f32[4,18,18,128]{3,2,1,0:T(8,128)S(1)} %scatter-add.31, f32[4,16,16,128]{3,2,1,0:T(8,128)} %add_select_fusion, s32[]{:T(128)} %constant.283.clone.1, s32[]{:T(128)} %bitcast.24, s32[]{:T(128)} %bitcast.25, s32[]{:T(128)} %constant.283.clone.1) | dynamic-update-slice | bytes 1048580 | tf_op jit(solution)/shard_map/scatter-add | solution.py:74
  75.8 1.1 fusion.1
  77.0 0.9 slice_add_fusion.4
  77.9 3.0 %scatter-add.36 = f32[4,18,18,128]{3,2,1,0:T(8,128)S(1)} dynamic-update-slice(f32[4,18,18,128]{3,2,1,0:T(8,128)S(1)} %fusion.1, f32[4,16,16,128]{3,2,1,0:T(8,128)} %slice_add_fusion.4, s32[]{:T(128)} %constant.283.clone.1, s32[]{:T(128)} %constant.292.clone.1, s32[]{:T(128)} %constant.292.clone.1, s32[]{:T(128)} %constant.283.clone.1) | dynamic-update-slice | bytes 1048580 | tf_op jit(solution)/shard_map/scatter-add | solution.py:74
  81.0 1.7 scatter-add.39
  82.8 1.7 scatter-add.41
  84.6 1.7 scatter-add.44
  86.3 0.8 fusion.5
  87.0 206.2 %all-reduce.6.cloned.1.call-done = f32[3456,128]{1,0:T(8,128)} async-done(((f32[3456,128]{1,0:T(8,128)}), f32[3456,128]{1,0:T(8,128)}) %all-reduce.6.cloned.1.call-update) | async-done | bytes 1769488 | tf_op jit(solution)/shard_map/psum | solution.py:77
  293.3 1.5 constant_dynamic-slice_fusion
  (61 shorter events, 5.5 us)
Async XLA Ops:
  7.2 7.2 %copy-start = (bf16[1,4,16,16,128]{4,3,2,1,0:T(8,128)(2,1)S(1)}, bf16[1,4,16,16,128]{4,3,2,1,0:T(8,128)(2,1)}, u32[]{:S(2)}) copy-start(bf16[1,4,16,16,128]{4,3,2,1,0:T(8,128)(2,1)} %param.22) | copy-start | bytes 786436
  7.2 286.1 %all-reduce.6.cloned.1.call-start = ((), (), s32[]{:S(2)}) async-start(), calls=%async_computation | async-start | bytes 3538944 | tf_op jit(solution)/shard_map/psum | solution.py:77
  8.2 8.4 %collective-permute-start = (bf16[1,2,16,16,128]{4,3,2,1,0:T(8,128)(2,1)S(1)}, bf16[1,2,16,16,128]{4,3,2,1,0:T(8,128)(2,1)S(1)}, u32[]{:S(2)}, u32[]{:S(2)}) collective-permute-start(bf16[1,2,16,16,128]{4,3,2,1,0:T(8,128)(2,1)S(1)} %slice.482), channel_id=1, source_target_pairs={{0,1},{1,2},{2,3},{3,4},{4,5},{5,6},{6,7},{7,8},{8,9},{9,10},{10,1... | collective-permute-start | bytes 393224 | tf_op jit(solution)/shard_map/ppermute | solution.py:10
  13.5 1.2 copy-start.2
  17.6 1.2 copy-start.1
  19.5 1.0 copy-start.3
  24.6 8.1 %collective-permute-start.1 = (bf16[1,2,16,16,128]{4,3,2,1,0:T(8,128)(2,1)S(1)}, bf16[1,2,16,16,128]{4,3,2,1,0:T(8,128)(2,1)S(1)}, u32[]{:S(2)}, u32[]{:S(2)}) collective-permute-start(bf16[1,2,16,16,128]{4,3,2,1,0:T(8,128)(2,1)S(1)} %slice.545), channel_id=1, source_target_pairs={{1,0},{2,1},{3,2},{4,3},{5,4},{6,5},{7,6},{8,7},{9,8},{10,9},{11,1... | collective-permute-start | bytes 393224 | tf_op jit(solution)/shard_map/ppermute | solution.py:10
Sparse Core Ops, SparseCore 0:
  31.9 261.3 all-reduce.5
where the time goes:
time: 302 us
  waiting for transfers between devices  207 us (69%)
  local copies, waits for them, and re-layouts  50.1 us (17%)
  between operations  14.5 us (5%)
  other arithmetic  11.7 us (4%)
  matrix products  10.2 us (3%)
  starting transfers between devices  7.76 us (3%)
    psum x1, waiting for transfers between devices, per_device(): total = lax.psum(grad_local, ('dp', 'tm'))  206 us
    scatter-add x7, local copies, waits for them, and re-layouts, per_device(): canvas.at[:, ky:ky + hh, kx:kx + ww].add(summed[:, :, :, ky * 3 + kx])  16.8 us
    slice x1, local copies, waits for them, and re-layouts, per_device(): summed[:, :, :, ky * 3 + kx]  16.6 us
    ppermute x2, starting transfers between devices, from_behind(): lax.ppermute(value, axis, [(source, source + steps) for source in range(l...  7.72 us
    reshape x1, local copies, waits for them, and re-layouts, per_device(): summed = summed.reshape(nfr, hh, ww, 9, cc)  6.85 us
  transfers between devices with their start and end apart: 3, of which 3 were waited for; matrix products, arithmetic and copies ran while one was open for 20% of the time, Pallas kernels for 0%

commit v1 on v0

--- a/solution.py
+++ b/solution.py
@@ -74,7 +74,9 @@
             canvas = canvas.at[:, ky : ky + hh, kx : kx + ww].add(summed[:, :, :, ky * 3 + kx])
     grad_clips = canvas[:, 1:-1, 1:-1].astype(jnp.bfloat16).reshape(clips.shape)
     share_rows = grad_local.shape[0] // lax.axis_size("tm")
-    total = lax.psum(grad_local, ("dp", "tm"))
+    total = grad_local
+    for name in ("tm", "dp"):
+        total = lax.psum(total, name)
     grad_weight = lax.dynamic_slice_in_dim(total, lax.axis_index("tm") * share_rows, share_rows, 0)
     return (activated, grad_clips, grad_weight)
 

time: 302 us -> 240 us (0.79)
  waiting for transfers between devices: 207 us -> 145 us
    psum x1 -> x2, waiting for transfers between devices: 206 us -> 144 us  [per_device(): total = lax.psum(total, name)]
  transfers between devices with their start and end apart: 3 -> 4, of which waited for: 3 -> 4; matrix products, arithmetic and copies ran while one was open for 20% -> 26% of each run, Pallas kernels for 0% -> 0%
where the time goes in v1:
time: 240 us; the launch traced here: 239 us
  waiting for transfers between devices  145 us (60%)
  local copies, waits for them, and re-layouts  50.1 us (21%)
  between operations  14.5 us (6%)
  other arithmetic  11.7 us (5%)
  matrix products  10.2 us (4%)
  starting transfers between devices  7.8 us (3%)
    psum x2, waiting for transfers between devices, per_device(): total = lax.psum(total, name)  144 us
    scatter-add x7, local copies, waits for them, and re-layouts, per_device(): canvas.at[:, ky:ky + hh, kx:kx + ww].add(summed[:, :, :, ky * 3 + kx])  16.8 us
    slice x1, local copies, waits for them, and re-layouts, per_device(): summed[:, :, :, ky * 3 + kx]  16.6 us
    ppermute x2, starting transfers between devices, from_behind(): lax.ppermute(value, axis, [(source, source + steps) for source in range(l...  7.54 us
    reshape x1, local copies, waits for them, and re-layouts, per_device(): summed = summed.reshape(nfr, hh, ww, 9, cc)  6.85 us
  transfers between devices with their start and end apart: 4, of which 4 were waited for; matrix products, arithmetic and copies ran while one was open for 26% of the time, Pallas kernels for 0%

profile of v1, /device:TPU:2, one launch (start us, length us, event | category | flops | bytes accessed | tf_op | source)
XLA Modules:
  0.0 239.1 jit_solution(17300621908931000470)
XLA Ops:
  7.2 0.9 slice.482
  8.2 1.9 collective-permute-start
  10.1 0.7 pad_add_fusion
  11.0 2.5 %pad_slice_fusion = (bf16[4,16,16,128]{3,2,1,0:T(8,128)(2,1)S(1)}, bf16[4,16,16,128]{3,2,1,0:T(8,128)(2,1)S(1)}, bf16[4,16,16,128]{3,2,1,0:T(8,128)(2,1)S(1)}, b...) fusion(bf16[4,16,16,128]{3,2,1,0:T(8,128)(2,1)} %bitcast.81), kind=kLoop, calls=%fused_computation.6 | loop fusion | bytes 2359296 | tf_op jit(solution)/shard_map/slice | solution.py:33
  18.7 0.8 fusion.30
  19.5 0.8 convolution_add_fusion.3
  20.5 1.6 fusion.3
  22.1 0.8 fusion.37
  22.9 0.8 fusion.36
  23.7 0.8 fusion.35
  24.6 5.6 %collective-permute-start.1 = (bf16[1,2,16,16,128]{4,3,2,1,0:T(8,128)(2,1)S(1)}, bf16[1,2,16,16,128]{4,3,2,1,0:T(8,128)(2,1)S(1)}, u32[]{:S(2)}, u32[]{:S(2)}) collective-permute-start(bf16[1,2,16,16,128]{4,3,2,1,0:T(8,128)(2,1)S(1)} %slice.545), channel_id=1, source_target_pairs={{1,0},{2,1},{3,2},{4,3},{5,4},{6,5},{7,6},{8,7},{9,8},{10,9},{11,1... | collective-permute-start | bytes 393224 | tf_op jit(solution)/shard_map/ppermute | solution.py:10
  30.2 1.3 maximum_multiply_fusion
  31.8 0.9 collective-permute-done.1
  33.0 0.8 fusion.28
  34.0 0.8 convolution_add_fusion.1
  34.7 3.0 %convolution_add_fusion = f32[1024,1152]{1,0:T(8,128)} fusion(f32[1024,1152]{1,0:T(8,128)S(1)} %convolution_add_fusion.1, bf16[1024,128]{1,0:T(8,128)(2,1)S(1)} %get-tuple-element.120, bf16[3456,128]{1,0:T(8,128)(2,1)S(1)} %copy-done.1), kind=kOutput, calls=%fused_computation | convolution fusion | flops 303169536 | bytes 9994240 | tf_op jit(solution)/shard_map/dot_general | solution.py:64
  37.7 6.9 %reshape.439 = f32[4,16,16,9,128]{4,3,2,1,0:T(8,128)} reshape(f32[1024,1152]{1,0:T(8,128)} %convolution_add_fusion) | data formatting | bytes 9437184 | tf_op jit(solution)/shard_map/reshape | solution.py:70
  44.6 16.6 %fusion.32 = (f32[4,16,16,1,128]{4,3,2,1,0:T(1,128)S(1)}, f32[4,16,16,1,128]{4,3,2,1,0:T(1,128)S(1)}, f32[4,16,16,1,128]{4,3,2,1,0:T(1,128)S(1)}, f32[4,16,16,1,...) fusion(f32[4,16,16,9,128]{4,3,2,1,0:T(8,128)} %reshape.439), kind=kLoop, calls=%fused_computation.101 | loop fusion | bytes 9437184 | tf_op jit(solution)/shard_map/slice | solution.py:74
  61.2 2.2 dynamic-slice_add_fusion
  63.4 4.3 %scatter-add.31 = f32[4,18,18,128]{3,2,1,0:T(8,128)S(1)} dynamic-update-slice(f32[4,18,18,128]{3,2,1,0:T(8,128)S(1)} %scatter-add.30, f32[4,16,16,128]{3,2,1,0:T(8,128)} %dynamic-slice_add_fusion, s32[]{:T(128)} %constant.283.clone.1, s32[]{:T(128)} %bitcast.21, s32[]{:T(128)} %bitcast.22, s32[]{:T(128)} %constant.283.clone.1) | dynamic-update-slice | bytes 1048580 | tf_op jit(solution)/shard_map/scatter-add | solution.py:74
  67.7 3.8 %add_select_fusion = f32[4,16,16,128]{3,2,1,0:T(8,128)} fusion(f32[4,16,16,128]{3,2,1,0:T(8,128)} %bitcast.89, f32[4,18,18,128]{3,2,1,0:T(8,128)S(1)} %scatter-add.31, s32[]{:T(128)} %bitcast.24, s32[]{:T(128)} %bitcast.25, pred[]{:T(512)} %and_reduce_fusion), kind=kLoop, calls=%fused_computation.5 | loop fusion | flops 262144 | bytes 1572873 | tf_op jit(solution)/shard_map/select.11
  71.5 4.3 %scatter-add.34 = f32[4,18,18,128]{3,2,1,0:T(8,128)S(1)} dynamic-update-slice(f32[4,18,18,128]{3,2,1,0:T(8,128)S(1)} %scatter-add.31, f32[4,16,16,128]{3,2,1,0:T(8,128)} %add_select_fusion, s32[]{:T(128)} %constant.283.clone.1, s32[]{:T(128)} %bitcast.24, s32[]{:T(128)} %bitcast.25, s32[]{:T(128)} %constant.283.clone.1) | dynamic-update-slice | bytes 1048580 | tf_op jit(solution)/shard_map/scatter-add | solution.py:74
  75.8 72.3 %all-reduce.7.cloned.1.call-done = f32[3456,128]{1,0:T(8,128)} async-done(((f32[3456,128]{1,0:T(8,128)}), f32[3456,128]{1,0:T(8,128)}) %all-reduce.7.cloned.1.call-update) | async-done | bytes 1769488 | tf_op jit(solution)/shard_map/psum | solution.py:79
  148.2 1.1 fusion.1
  149.3 0.9 slice_add_fusion.4
  150.2 3.0 %scatter-add.36 = f32[4,18,18,128]{3,2,1,0:T(8,128)S(1)} dynamic-update-slice(f32[4,18,18,128]{3,2,1,0:T(8,128)S(1)} %fusion.1, f32[4,16,16,128]{3,2,1,0:T(8,128)} %slice_add_fusion.4, s32[]{:T(128)} %constant.283.clone.1, s32[]{:T(128)} %constant.292.clone.1, s32[]{:T(128)} %constant.292.clone.1, s32[]{:T(128)} %constant.283.clone.1) | dynamic-update-slice | bytes 1048580 | tf_op jit(solution)/shard_map/scatter-add | solution.py:74
  153.3 1.7 scatter-add.39
  155.2 1.7 scatter-add.41
  156.9 1.7 scatter-add.44
  158.6 0.8 fusion.5
  159.4 71.5 %all-reduce.9.cloned.1.call-done = f32[3456,128]{1,0:T(8,128)} async-done(((f32[3456,128]{1,0:T(8,128)}), f32[3456,128]{1,0:T(8,128)}) %all-reduce.9.cloned.1.call-update) | async-done | bytes 1769488 | tf_op jit(solution)/shard_map/psum | solution.py:79
  230.8 1.5 constant_dynamic-slice_fusion
  (64 shorter events, 6.5 us)
Async XLA Ops:
  7.2 7.2 %copy-start = (bf16[1,4,16,16,128]{4,3,2,1,0:T(8,128)(2,1)S(1)}, bf16[1,4,16,16,128]{4,3,2,1,0:T(8,128)(2,1)}, u32[]{:S(2)}) copy-start(bf16[1,4,16,16,128]{4,3,2,1,0:T(8,128)(2,1)} %param.22) | copy-start | bytes 786436
  7.2 141.0 %all-reduce.7.cloned.1.call-start = ((), (), s32[]{:S(2)}) async-start(), calls=%async_computation | async-start | bytes 3538944 | tf_op jit(solution)/shard_map/psum | solution.py:79
  8.2 8.4 %collective-permute-start = (bf16[1,2,16,16,128]{4,3,2,1,0:T(8,128)(2,1)S(1)}, bf16[1,2,16,16,128]{4,3,2,1,0:T(8,128)(2,1)S(1)}, u32[]{:S(2)}, u32[]{:S(2)}) collective-permute-start(bf16[1,2,16,16,128]{4,3,2,1,0:T(8,128)(2,1)S(1)} %slice.482), channel_id=1, source_target_pairs={{0,1},{1,2},{2,3},{3,4},{4,5},{5,6},{6,7},{7,8},{8,9},{9,10},{10,1... | collective-permute-start | bytes 393224 | tf_op jit(solution)/shard_map/ppermute | solution.py:10
  13.5 1.2 copy-start.2
  17.6 1.2 copy-start.1
  19.5 1.0 copy-start.3
  24.6 8.1 %collective-permute-start.1 = (bf16[1,2,16,16,128]{4,3,2,1,0:T(8,128)(2,1)S(1)}, bf16[1,2,16,16,128]{4,3,2,1,0:T(8,128)(2,1)S(1)}, u32[]{:S(2)}, u32[]{:S(2)}) collective-permute-start(bf16[1,2,16,16,128]{4,3,2,1,0:T(8,128)(2,1)S(1)} %slice.545), channel_id=1, source_target_pairs={{1,0},{2,1},{3,2},{4,3},{5,4},{6,5},{7,6},{8,7},{9,8},{10,9},{11,1... | collective-permute-start | bytes 393224 | tf_op jit(solution)/shard_map/ppermute | solution.py:10
  31.6 199.3 %all-reduce.9.cloned.1.call-start = ((), (), s32[]{:S(2)}) async-start(), calls=%async_computation.1 | async-start | bytes 3538944 | tf_op jit(solution)/shard_map/psum | solution.py:79
Sparse Core Ops, SparseCore 0:
  31.7 116.4 all-reduce.6
  150.5 80.2 all-reduce.8
